TPU v7x, 256 devices: a whole 4x4x8 slice. The times are simulated.
256 devices in a mesh: row: 32 (over y, x, core), col: 8 (over z).
Axes of the slice: x: 4, y: 4, z: 8, core: 2. Of those that a mesh axis runs over, the one named last changes fastest.
Arguments:
- covariance: float32 [8192, 8192], P('row', 'col'), may hold values from 0 to 4, as said below
- panels: int32 [4], replicated, may hold values from 0 to 31, as said below
- observed: float32 [8192], P('row'), may hold values from -6 to 6
- drift_basis: float32 [64, 8192], P(None, 'row'), may hold values from -1.5 to 1.5
Outputs:
- complement: float32 [8192, 8192], P('row', 'col')
- factor: float32 [8192, 1024], P('row')
- solved_data: float32 [8192], P('row')
- solved_drift: float32 [64, 8192], P(None, 'row')
Inputs may be any that keep to these rules, and one draw needn't show every extreme that they name: `covariance`: symmetric and positive definite. `panels`: 4 different tile indices; tile 32 - 1 is always among them.
All inputs are finite; a program needn't handle non-finite values.
Results may differ from a plain program's by a relative error of at most 0.0003.
Values sent between devices are 32-bit elements; how exact they have to be, the bound alone decides.
No kernel may reach another device: no remote copies, remote signals or barrier semaphores. Data moves between devices by JAX's collectives and lax.ppermute only.
A program may use at most 64 MiB of HBM per device.

v0:
```python
import jax
import jax.numpy as jnp
from jax import lax
from jax.sharding import PartitionSpec as P

B = 256
K = 4


def from_root(value, axis, root):
    return lax.dynamic_index_in_dim(lax.all_gather(value, axis), root, 0, keepdims=False)


def broadcast(value, axis, root):
    mine = lax.axis_index(axis) == root
    return lax.psum(jnp.where(mine, value, jnp.zeros_like(value)), axis)


def solve_right(chol_tile, values):
    return lax.linalg.triangular_solve(
        chol_tile, values, left_side=False, lower=True, transpose_a=True
    )


def keep_mask(tiles, chosen):
    return jnp.all(tiles[:, None] != chosen[None, :], axis=1).astype(jnp.float32)


def outer_product(rows_factor, cols_factor):
    return lax.dot_general(
        rows_factor, cols_factor, (((1,), (0,)), ((), ())), precision=lax.Precision.HIGHEST
    )


def on_device(covariance, panels, observed, drift_basis):
    rows_here = covariance.shape[0]
    cols_here = covariance.shape[1]
    row_start = lax.axis_index("row") * rows_here
    col_start = lax.axis_index("col") * cols_here
    row_tiles = (row_start + lax.iota(jnp.int32, rows_here)) // B
    col_tiles = (col_start + lax.iota(jnp.int32, cols_here)) // B
    sides = jnp.concatenate([observed[None, :], drift_basis], axis=0)
    matrix = covariance
    factors = []
    for position in range(K):
        target = panels[position]
        offset = target * B
        row_owner = offset // rows_here
        col_owner = offset // cols_here
        col_off = offset - col_owner * cols_here
        keep_rows = keep_mask(row_tiles, panels[:position])
        keep_cols = keep_mask(col_tiles, panels[:position])
        col_slab = lax.dynamic_slice_in_dim(matrix, col_off, B, 1)
        col_slab = from_root(col_slab, "col", col_owner)
        side_tile = sides
        diag_tile = col_slab
        row_slab = matrix
        row_slab, diag_tile, side_tile = (
            broadcast(row_slab, "row", row_owner),
            broadcast(diag_tile, "row", row_owner),
            broadcast(side_tile, "row", row_owner),
        )
        chol_tile = jnp.linalg.cholesky(diag_tile)
        rows_factor = solve_right(chol_tile, col_slab) * keep_rows[:, None]
        cols_factor = (
            lax.linalg.triangular_solve(
                chol_tile, row_slab, left_side=True, lower=True, transpose_a=False
            )
            * keep_cols[None, :]
        )
        solved = solve_right(chol_tile, side_tile)
        matrix = matrix - outer_product(rows_factor, cols_factor)
        sides = sides - lax.dot_general(
            solved, rows_factor, (((1,), (1,)), ((), ())), precision=lax.Precision.HIGHEST
        )
        sides = jnp.where((row_tiles == target)[None, :], solved, sides)
        factors.append(rows_factor)
    final_rows = keep_mask(row_tiles, panels)
    final_cols = keep_mask(col_tiles, panels)
    complement = matrix * final_rows[:, None] * final_cols[None, :]
    return (complement, jnp.concatenate(factors, axis=1), sides[0], sides[1:])


def solution(mesh):
    return jax.shard_map(
        on_device,
        mesh=mesh,
        in_specs=(P("row", "col"), P(), P("row"), P(None, "row")),
        out_specs=(P("row", "col"), P("row", None), P("row"), P(None, "row")),
        check_vma=False,
    )
```

profile of v0, /device:TPU:6, one launch (start us, length us, event | category | flops | bytes accessed | tf_op | source)
XLA Modules:
  0.0 943.6 jit_solution(15376847191350219697)
XLA Ops:
  7.2 1.4 fusion.110
  9.3 1.7 constant_dynamic-slice_fusion.11
  11.1 1.5 fusion.62
  12.6 1.1 broadcast_select_fusion.3
  13.6 41.5 %all-gather.9.cloned.1.call-done = f32[2048,256]{1,0:T(8,128)} async-done(((f32[256,256]{1,0:T(8,128)}), f32[2048,256]{1,0:T(8,128)}) %all-gather.9.cloned.1.call-update) | async-done | bytes 2097168 | tf_op jit(solution)/shard_map/all_gather | solution.py:11
  55.2 1.0 constant_dynamic-slice_fusion.10
  57.8 117.0 %all-reduce.16.cloned.1.call-done = (f32[256,1024]{1,0:T(8,128)}, f32[256,256]{0,1:T(8,128)}, f32[65,256]{1,0:T(8,128)}) async-done(((f32[256,1024]{1,0:T(8,128)}, f32[256,256]{0,1:T(8,128)}, f32[65,256]{1,0:T(8,128)}), (f32[256,1024]{1,0:T(8,128)}, f32[256,256]{0,1:T(8,128)}, f32[65,256]{1,0:T(8,128)})) %all-reduce.16.cloned.1.call-update) | async-done | bytes 1377296 | tf_op jit(solution)/shard_map/psum | solution.py:16
  174.8 1.1 copy.18
  175.9 1.0 fusion.29
  176.9 11.7 %cholesky.214 = f32[128,128]{1,0:T(8,128)S(1)} custom-call(f32[128,128]{1,0:T(8,128)S(1)} %cholesky.346), custom_call_target="Cholesky" | custom-call | tf_op jit(solution)/shard_map/jit(cholesky)/cholesky | solution.py:63
  188.6 9.8 %custom-call.29 = f32[1,128,128]{1,2,0:T(8,128)S(1)} custom-call(f32[1,128,128]{2,1,0:T(8,128)S(1)} %get-tuple-element.173), custom_call_target="InvertDiagBlocksLowerTriangular" | custom-call | tf_op jit(solution)/shard_map/jit(cholesky)/cholesky | solution.py:63
  198.9 11.7 %cholesky.231 = f32[128,128]{1,0:T(8,128)S(1)} custom-call(f32[128,128]{1,0:T(8,128)S(1)} %convolution_subtract_fusion.19), custom_call_target="Cholesky" | custom-call | tf_op jit(solution)/shard_map/jit(cholesky)/cholesky | solution.py:63
  212.8 4.2 while.24
  213.6 1.4 bitcast_dynamic-update-slice_fusion.8
  215.6 1.4 bitcast_dynamic-update-slice_fusion.8
  217.0 19.7 %custom-call.30 = f32[2,128,128]{1,2,0:T(8,128)S(1)} custom-call(f32[2,128,128]{2,1,0:T(8,128)S(1)} %get-tuple-element.86), custom_call_target="InvertDiagBlocksLowerTriangular" | custom-call | tf_op jit(solution)/shard_map/triangular_solve/custom-call.0 | solution.py:20
  238.2 1.6 convolution_subtract_fusion.7
  240.5 2.1 broadcast_select_fusion.2
  245.7 37.7 %all-gather.11.cloned.1.call-done = f32[2048,256]{1,0:T(8,128)} async-done(((f32[256,256]{1,0:T(8,128)}), f32[2048,256]{1,0:T(8,128)}) %all-gather.11.cloned.1.call-update) | async-done | bytes 2097168 | tf_op jit(solution)/shard_map/all_gather | solution.py:11
  283.4 1.0 constant_dynamic-slice_fusion.8
  286.2 1.3 compare_convert_fusion.1
  288.2 114.5 %all-reduce.14.cloned.1.call-done = (f32[256,256]{0,1:T(8,128)}, f32[256,1024]{1,0:T(8,128)}, f32[65,256]{1,0:T(8,128)}) async-done(((f32[256,256]{0,1:T(8,128)}, f32[256,1024]{1,0:T(8,128)}, f32[65,256]{1,0:T(8,128)}), (f32[256,256]{0,1:T(8,128)}, f32[256,1024]{1,0:T(8,128)}, f32[65,256]{1,0:T(8,128)})) %all-reduce.14.cloned.1.call-update) | async-done | bytes 1377296 | tf_op jit(solution)/shard_map/psum | solution.py:16
  402.7 1.1 copy.20
  403.8 1.0 fusion.28
  404.8 11.7 %cholesky.248 = f32[128,128]{1,0:T(8,128)S(1)} custom-call(f32[128,128]{1,0:T(8,128)S(1)} %cholesky.349), custom_call_target="Cholesky" | custom-call | tf_op jit(solution)/shard_map/jit(cholesky)/cholesky | solution.py:63
  416.6 9.8 %custom-call.32 = f32[1,128,128]{1,2,0:T(8,128)S(1)} custom-call(f32[1,128,128]{2,1,0:T(8,128)S(1)} %get-tuple-element.169), custom_call_target="InvertDiagBlocksLowerTriangular" | custom-call | tf_op jit(solution)/shard_map/jit(cholesky)/cholesky | solution.py:63
  426.9 11.7 %cholesky.265 = f32[128,128]{1,0:T(8,128)S(1)} custom-call(f32[128,128]{1,0:T(8,128)S(1)} %convolution_subtract_fusion.18), custom_call_target="Cholesky" | custom-call | tf_op jit(solution)/shard_map/jit(cholesky)/cholesky | solution.py:63
  441.3 4.5 while.25
  442.3 1.4 bitcast_dynamic-update-slice_fusion.9
  444.3 1.4 bitcast_dynamic-update-slice_fusion.9
  445.7 19.7 %custom-call.33 = f32[2,128,128]{1,2,0:T(8,128)S(1)} custom-call(f32[2,128,128]{2,1,0:T(8,128)S(1)} %get-tuple-element.88), custom_call_target="InvertDiagBlocksLowerTriangular" | custom-call | tf_op jit(solution)/shard_map/triangular_solve/custom-call.0 | solution.py:20
  466.4 1.7 fusion.19
  468.0 1.6 convolution_subtract_fusion.6
  470.3 2.1 broadcast_select_fusion.1
  474.9 38.3 %all-gather.13.cloned.1.call-done = f32[2048,256]{1,0:T(8,128)} async-done(((f32[256,256]{1,0:T(8,128)}), f32[2048,256]{1,0:T(8,128)}) %all-gather.13.cloned.1.call-update) | async-done | bytes 2097168 | tf_op jit(solution)/shard_map/all_gather | solution.py:11
  513.2 1.0 constant_dynamic-slice_fusion.6
  516.7 115.8 %all-reduce.12.cloned.1.call-done = (f32[256,256]{0,1:T(8,128)}, f32[256,1024]{1,0:T(8,128)}, f32[65,256]{1,0:T(8,128)}) async-done(((f32[256,256]{0,1:T(8,128)}, f32[256,1024]{1,0:T(8,128)}, f32[65,256]{1,0:T(8,128)}), (f32[256,256]{0,1:T(8,128)}, f32[256,1024]{1,0:T(8,128)}, f32[65,256]{1,0:T(8,128)})) %all-reduce.12.cloned.1.call-update) | async-done | bytes 1377296 | tf_op jit(solution)/shard_map/psum | solution.py:16
  632.5 1.1 copy.22
  633.6 1.0 fusion.27
  634.6 11.7 %cholesky.282 = f32[128,128]{1,0:T(8,128)S(1)} custom-call(f32[128,128]{1,0:T(8,128)S(1)} %cholesky.352), custom_call_target="Cholesky" | custom-call | tf_op jit(solution)/shard_map/jit(cholesky)/cholesky | solution.py:63
  646.9 9.8 %custom-call.35 = f32[1,128,128]{1,2,0:T(8,128)S(1)} custom-call(f32[1,128,128]{2,1,0:T(8,128)S(1)} %get-tuple-element.165), custom_call_target="InvertDiagBlocksLowerTriangular" | custom-call | tf_op jit(solution)/shard_map/jit(cholesky)/cholesky | solution.py:63
  657.2 11.7 %cholesky.299 = f32[128,128]{1,0:T(8,128)S(1)} custom-call(f32[128,128]{1,0:T(8,128)S(1)} %convolution_subtract_fusion.17), custom_call_target="Cholesky" | custom-call | tf_op jit(solution)/shard_map/jit(cholesky)/cholesky | solution.py:63
  669.6 1.3 compare_reduce_fusion.9
  672.2 5.6 while.26
  673.7 1.4 bitcast_dynamic-update-slice_fusion.10
  676.4 1.4 bitcast_dynamic-update-slice_fusion.10
  677.8 19.7 %custom-call.36 = f32[2,128,128]{1,2,0:T(8,128)S(1)} custom-call(f32[2,128,128]{2,1,0:T(8,128)S(1)} %get-tuple-element.90), custom_call_target="InvertDiagBlocksLowerTriangular" | custom-call | tf_op jit(solution)/shard_map/triangular_solve/custom-call.0 | solution.py:20
  700.3 2.1 broadcast_select_fusion
  705.5 37.7 %all-gather.15.cloned.1.call-done = f32[2048,256]{1,0:T(8,128)} async-done(((f32[256,256]{1,0:T(8,128)}), f32[2048,256]{1,0:T(8,128)}) %all-gather.15.cloned.1.call-update) | async-done | bytes 2097168 | tf_op jit(solution)/shard_map/all_gather | solution.py:11
  746.0 1.1 broadcast_compare_fusion.2
  747.1 115.5 %all-reduce.10.cloned.1.call-done = (f32[256,256]{0,1:T(8,128)}, f32[256,1024]{1,0:T(8,128)}, f32[65,256]{1,0:T(8,128)}) async-done(((f32[256,256]{0,1:T(8,128)}, f32[256,1024]{1,0:T(8,128)}, f32[65,256]{1,0:T(8,128)}), (f32[256,256]{0,1:T(8,128)}, f32[256,1024]{1,0:T(8,128)}, f32[65,256]{1,0:T(8,128)})) %all-reduce.10.cloned.1.call-update) | async-done | bytes 1377296 | tf_op jit(solution)/shard_map/psum | solution.py:16
  862.7 1.1 copy.24
  863.8 1.0 fusion.26
  864.8 11.7 %cholesky.316 = f32[128,128]{1,0:T(8,128)S(1)} custom-call(f32[128,128]{1,0:T(8,128)S(1)} %cholesky.355), custom_call_target="Cholesky" | custom-call | tf_op jit(solution)/shard_map/jit(cholesky)/cholesky | solution.py:63
  876.6 9.8 %custom-call.38 = f32[1,128,128]{1,2,0:T(8,128)S(1)} custom-call(f32[1,128,128]{2,1,0:T(8,128)S(1)} %get-tuple-element.161), custom_call_target="InvertDiagBlocksLowerTriangular" | custom-call | tf_op jit(solution)/shard_map/jit(cholesky)/cholesky | solution.py:63
  886.9 11.7 %cholesky.333 = f32[128,128]{1,0:T(8,128)S(1)} custom-call(f32[128,128]{1,0:T(8,128)S(1)} %convolution_subtract_fusion.16), custom_call_target="Cholesky" | custom-call | tf_op jit(solution)/shard_map/jit(cholesky)/cholesky | solution.py:63
  901.2 4.3 while.27
  902.1 1.4 bitcast_dynamic-update-slice_fusion.11
  904.1 1.4 bitcast_dynamic-update-slice_fusion.11
  905.5 19.7 %custom-call.39 = f32[2,128,128]{1,2,0:T(8,128)S(1)} custom-call(f32[2,128,128]{2,1,0:T(8,128)S(1)} %get-tuple-element.92), custom_call_target="InvertDiagBlocksLowerTriangular" | custom-call | tf_op jit(solution)/shard_map/triangular_solve/custom-call.0 | solution.py:20
  929.0 1.3 copy.25
  930.3 1.7 fusion.15
  932.0 1.6 convolution_subtract_fusion.4
  934.3 2.1 fusion.1
  (172 shorter events, 39.8 us)
Async XLA Ops:
  7.2 48.0 %all-gather.9.cloned.1.call-start = ((), (), s32[]{:S(2)}) async-start(), calls=%async_computation | async-start | bytes 2359296 | tf_op jit(solution)/shard_map/all_gather | solution.py:11
  11.0 163.8 %all-reduce.16.cloned.1.call-start = ((), (), s32[]{:S(2)}) async-start(), calls=%async_computation.7 | async-start | bytes 2768896 | tf_op jit(solution)/shard_map/psum | solution.py:16
  57.0 226.4 %all-gather.11.cloned.1.call-start = ((), (), s32[]{:S(2)}) async-start(), calls=%async_computation.1 | async-start | bytes 2359296 | tf_op jit(solution)/shard_map/all_gather | solution.py:11
  176.8 60.7 %copy-start.2 = (f32[256,1024]{1,0:T(8,128)S(1)}, f32[256,1024]{1,0:T(8,128)}, u32[]{:S(2)}) copy-start(f32[256,1024]{1,0:T(8,128)} %get-tuple-element.147) | copy-start | bytes 3145732
  237.3 3.3 copy-start
  240.5 3.6 copy-start.7
  240.5 4.3 copy-start.4
  240.5 4.3 copy-start.10
  243.3 159.4 %all-reduce.14.cloned.1.call-start = ((), (), s32[]{:S(2)}) async-start(), calls=%async_computation.6 | async-start | bytes 2768896 | tf_op jit(solution)/shard_map/psum | solution.py:16
  285.3 227.9 %all-gather.13.cloned.1.call-start = ((), (), s32[]{:S(2)}) async-start(), calls=%async_computation.2 | async-start | bytes 2359296 | tf_op jit(solution)/shard_map/all_gather | solution.py:11
  445.7 20.6 %copy-start.13 = (s32[2,2]{1,0:T(2,128)}, s32[2,2]{1,0:T(2,128)S(1)}, u32[]{:S(2)}) copy-start(s32[2,2]{1,0:T(2,128)S(1)} %get-tuple-element.455) | copy-start | bytes 52
  470.3 2.9 copy-start.6
  473.1 42.7 %copy-start.9 = (s32[4]{0:T(128)S(1)}, s32[4]{0:T(128)}, u32[]{:S(2)}) copy-start(s32[4]{0:T(128)} %param.12) | copy-start | bytes 52
  473.1 159.4 %all-reduce.12.cloned.1.call-start = ((), (), s32[]{:S(2)}) async-start(), calls=%async_computation.5 | async-start | bytes 2768896 | tf_op jit(solution)/shard_map/psum | solution.py:16
  515.0 228.2 %all-gather.15.cloned.1.call-start = ((), (), s32[]{:S(2)}) async-start(), calls=%async_computation.3 | async-start | bytes 2359296 | tf_op jit(solution)/shard_map/all_gather | solution.py:11
  634.6 63.8 %copy-start.1 = (f32[256,1024]{1,0:T(8,128)S(1)}, f32[256,1024]{1,0:T(8,128)}, u32[]{:S(2)}) copy-start(f32[256,1024]{1,0:T(8,128)} %get-tuple-element.142) | copy-start | bytes 3145732
  698.1 2.2 copy-start.11
  700.3 3.5 copy-start.5
  700.3 4.2 copy-start.3
  703.1 159.5 %all-reduce.10.cloned.1.call-start = ((), (), s32[]{:S(2)}) async-start(), calls=%async_computation.4 | async-start | bytes 2768896 | tf_op jit(solution)/shard_map/psum | solution.py:16
  745.0 156.2 %copy-start.14 = (s32[2,2]{1,0:T(2,128)S(1)}, s32[2,2]{1,0:T(2,128)}, u32[]{:S(2)}) copy-start(s32[2,2]{1,0:T(2,128)} %get-tuple-element.456) | copy-start | bytes 52
  862.7 62.5 %copy-start.8 = (f32[65,256]{1,0:T(8,128)S(1)}, f32[65,256]{1,0:T(8,128)}, u32[]{:S(2)}) copy-start(f32[65,256]{1,0:T(8,128)} %get-tuple-element.140) | copy-start | bytes 199684
  876.5 50.3 %copy-start.12 = (f32[256]{0:T(256)S(1)}, f32[256]{0:T(256)}, u32[]{:S(2)}) copy-start(f32[256]{0:T(256)} %convert_element_type.60) | copy-start | bytes 3076
Sparse Core Ops, SparseCore 0:
  11.1 44.0 all-gather.8
  59.4 115.3 all-reduce.15
  243.5 39.8 all-gather.10
  287.5 115.1 all-reduce.13
  473.2 39.8 all-gather.12
  517.3 115.1 all-reduce.11
  703.3 39.8 all-gather.14
  747.4 115.1 all-reduce.9
where the time goes:
time: 953 us; the launch traced here: 944 us
  waiting for transfers between devices  618 us (65%)
  other arithmetic  233 us (24%)
  local copies, waits for them, and re-layouts  33.9 us (4%)
  matrix products  32.6 us (3%)
  between operations  23.3 us (2%)
    psum x4, waiting for transfers between devices, broadcast(): return lax.psum(jnp.where(mine, value, jnp.zeros_like(value)), axis)  463 us
    all_gather x4, waiting for transfers between devices, from_root(): lax.all_gather(value, axis)  155 us
    another operation x27, other arithmetic, on_device(): chol_tile = jnp.linalg.cholesky(diag_tile)  139 us
    another operation x9, other arithmetic, solve_right(): lax.linalg.triangular_solve(chol_tile, values, left_side=False, lower=Tru...  78.8 us
  transfers between devices with their start and end apart: 8, of which 8 were waited for; matrix products, arithmetic and copies ran while one was open for 1% of the time, Pallas kernels for 0%

commit v1 on v0

--- a/solution.py
+++ b/solution.py
@@ -13,7 +13,7 @@
 
 def broadcast(value, axis, root):
     mine = lax.axis_index(axis) == root
-    return lax.psum(jnp.where(mine, value, jnp.zeros_like(value)), axis)
+    return jnp.sum(lax.all_gather(jnp.where(mine, value, jnp.zeros_like(value)), axis), axis=0)
 
 
 def solve_right(chol_tile, values):

time: 953 us -> 1160 us (1.22)
  waiting for transfers between devices: 618 us -> 770 us
  other arithmetic: 233 us -> 303 us
    all_gather x0 -> x12, waiting for transfers between devices: none -> 605 us  [broadcast(): lax.all_gather(jnp.where(mine, value, jnp.zeros_like(value)), axis)]
    psum x4 -> x0, waiting for transfers between devices: 463 us -> none  [broadcast(): return lax.psum(jnp.where(mine, value, jnp.zeros_like(value)), axis)]
    reduce_sum x0 -> x12, other arithmetic: none -> 70.4 us  [broadcast(): jnp.sum(lax.all_gather(jnp.where(mine, value, jnp.zeros_like(value)), axi...]
  transfers between devices with their start and end apart: 8 -> 16, of which waited for: 8 -> 16; matrix products, arithmetic and copies ran while one was open for 1% -> 28% of each run, Pallas kernels for 0% -> 0%
where the time goes in v1:
time: 1160 us; the launch traced here: 1150 us
  waiting for transfers between devices  770 us (66%)
  other arithmetic  303 us (26%)
  matrix products  27.9 us (2%)
  local copies, waits for them, and re-layouts  24.4 us (2%)
  between operations  23.1 us (2%)
    all_gather x12, waiting for transfers between devices, broadcast(): lax.all_gather(jnp.where(mine, value, jnp.zeros_like(value)), axis)  605 us
    all_gather x4, waiting for transfers between devices, from_root(): lax.all_gather(value, axis)  163 us
    another operation x27, other arithmetic, on_device(): chol_tile = jnp.linalg.cholesky(diag_tile)  138 us
    another operation x9, other arithmetic, solve_right(): lax.linalg.triangular_solve(chol_tile, values, left_side=False, lower=Tru...  78.8 us
    reduce_sum x12, other arithmetic, broadcast(): jnp.sum(lax.all_gather(jnp.where(mine, value, jnp.zeros_like(value)), axi...  70.4 us
  transfers between devices with their start and end apart: 16, of which 16 were waited for; matrix products, arithmetic and copies ran while one was open for 28% of the time, Pallas kernels for 0%

profile of v1, /device:TPU:6, one launch (start us, length us, event | category | flops | bytes accessed | tf_op | source)
XLA Modules:
  0.0 1150.4 jit_solution(55648069791971921)
XLA Ops:
  7.2 1.5 fusion.109
  9.3 1.7 constant_dynamic-slice_fusion.7
  11.1 44.1 %all-gather.41.cloned.1.call-done = f32[2048,256]{1,0:T(8,128)} async-done(((f32[256,256]{1,0:T(8,128)}), f32[2048,256]{1,0:T(8,128)}) %all-gather.41.cloned.1.call-update) | async-done | bytes 2097168 | tf_op jit(solution)/shard_map/all_gather | solution.py:11
  55.2 1.7 dynamic-slice_bitcast_fusion.3
  58.7 56.1 %all-gather.31.cloned.1.call-done = f32[32,256,256]{2,1,0:T(8,128)} async-done(((f32[1,256,256]{2,1,0:T(8,128)}), f32[32,256,256]{2,1,0:T(8,128)}) %all-gather.31.cloned.1.call-update) | async-done | bytes 8388624 | tf_op jit(solution)/shard_map/all_gather | solution.py:16
  114.8 3.9 reduce_sum.108
  118.9 11.7 %cholesky.214 = f32[128,128]{1,0:T(8,128)S(1)} custom-call(f32[128,128]{1,0:T(8,128)S(1)} %cholesky.346), custom_call_target="Cholesky" | custom-call | tf_op jit(solution)/shard_map/jit(cholesky)/cholesky | solution.py:63
  130.6 9.8 custom-call.29
  141.0 11.7 %cholesky.231 = f32[128,128]{1,0:T(8,128)S(1)} custom-call(f32[128,128]{1,0:T(8,128)S(1)} %convolution_subtract_fusion.19), custom_call_target="Cholesky" | custom-call | tf_op jit(solution)/shard_map/jit(cholesky)/cholesky | solution.py:63
  154.9 4.3 while.24
  155.7 1.4 bitcast_dynamic-update-slice_fusion.8
  157.7 1.4 bitcast_dynamic-update-slice_fusion.8
  159.2 19.7 %custom-call.30 = f32[2,128,128]{1,2,0:T(8,128)S(1)} custom-call(f32[2,128,128]{2,1,0:T(8,128)S(1)} %get-tuple-element.86), custom_call_target="InvertDiagBlocksLowerTriangular" | custom-call | tf_op jit(solution)/shard_map/triangular_solve/custom-call.0 | solution.py:20
  179.9 56.7 %all-gather.43.cloned.1.call-done = f32[8192,1024]{1,0:T(8,128)} async-done(((f32[256,1024]{1,0:T(8,128)}), f32[8192,1024]{1,0:T(8,128)}) %all-gather.43.cloned.1.call-update) | async-done | bytes 33554448 | tf_op jit(solution)/shard_map/all_gather | solution.py:16
  236.7 11.8 %reduce_sum.109 = f32[256,1024]{1,0:T(8,128)S(1)} reduce(f32[32,256,1024]{2,1,0:T(8,128)} %bitcast.244, f32[]{:T(128)} %constant.178.clone.1), dimensions={0}, to_apply=%region_5.8 | reduce | flops 8126464 | bytes 34603012 | tf_op jit(solution)/shard_map/reduce_sum | solution.py:16
  250.4 2.0 broadcast_select_fusion.2
  253.3 40.5 %all-gather.45.cloned.1.call-done = f32[2048,256]{1,0:T(8,128)} async-done(((f32[256,256]{1,0:T(8,128)}), f32[2048,256]{1,0:T(8,128)}) %all-gather.45.cloned.1.call-update) | async-done | bytes 2097168 | tf_op jit(solution)/shard_map/all_gather | solution.py:11
  293.8 1.7 dynamic-slice_select_fusion.2
  298.7 54.5 %all-gather.33.cloned.1.call-done = f32[32,256,256]{2,1,0:T(8,128)} async-done(((f32[1,256,256]{2,1,0:T(8,128)}), f32[32,256,256]{2,1,0:T(8,128)}) %all-gather.33.cloned.1.call-update) | async-done | bytes 8388624 | tf_op jit(solution)/shard_map/all_gather | solution.py:16
  353.2 3.9 reduce_sum.110
  357.3 11.7 %cholesky.248 = f32[128,128]{1,0:T(8,128)S(1)} custom-call(f32[128,128]{1,0:T(8,128)S(1)} %cholesky.349), custom_call_target="Cholesky" | custom-call | tf_op jit(solution)/shard_map/jit(cholesky)/cholesky | solution.py:63
  369.1 9.8 custom-call.32
  379.4 11.7 %cholesky.265 = f32[128,128]{1,0:T(8,128)S(1)} custom-call(f32[128,128]{1,0:T(8,128)S(1)} %convolution_subtract_fusion.18), custom_call_target="Cholesky" | custom-call | tf_op jit(solution)/shard_map/jit(cholesky)/cholesky | solution.py:63
  393.7 4.2 while.25
  397.9 19.7 %custom-call.33 = f32[2,128,128]{1,2,0:T(8,128)S(1)} custom-call(f32[2,128,128]{2,1,0:T(8,128)S(1)} %get-tuple-element.88), custom_call_target="InvertDiagBlocksLowerTriangular" | custom-call | tf_op jit(solution)/shard_map/triangular_solve/custom-call.0 | solution.py:20
  418.7 56.2 %all-gather.47.cloned.1.call-done = f32[8192,1024]{1,0:T(8,128)} async-done(((f32[256,1024]{1,0:T(8,128)}), f32[8192,1024]{1,0:T(8,128)}) %all-gather.47.cloned.1.call-update) | async-done | bytes 33554448 | tf_op jit(solution)/shard_map/all_gather | solution.py:16
  474.8 11.8 %reduce_sum.111 = f32[256,1024]{1,0:T(8,128)S(1)} reduce(f32[32,256,1024]{2,1,0:T(8,128)} %bitcast.243, f32[]{:T(128)} %constant.178.clone.1), dimensions={0}, to_apply=%region_7.11 | reduce | flops 8126464 | bytes 34603012 | tf_op jit(solution)/shard_map/reduce_sum | solution.py:16
  488.6 2.0 broadcast_select_fusion.1
  492.0 33.8 %all-gather.39.cloned.1.call-done = f32[32,65,256]{2,1,0:T(8,128)} async-done(((f32[1,65,256]{2,1,0:T(8,128)}), f32[32,65,256]{2,1,0:T(8,128)}) %all-gather.39.cloned.1.call-update) | async-done | bytes 2129936 | tf_op jit(solution)/shard_map/all_gather | solution.py:16
  525.8 1.8 reduce_sum.116
  530.2 38.9 %all-gather.49.cloned.1.call-done = f32[2048,256]{1,0:T(8,128)} async-done(((f32[256,256]{1,0:T(8,128)}), f32[2048,256]{1,0:T(8,128)}) %all-gather.49.cloned.1.call-update) | async-done | bytes 2097168 | tf_op jit(solution)/shard_map/all_gather | solution.py:11
  569.1 1.7 dynamic-slice_select_fusion.1
  573.1 46.0 %all-gather.57.cloned.1.call-done = f32[32,65,256]{2,1,0:T(8,128)} async-done(((f32[1,65,256]{2,1,0:T(8,128)}), f32[32,65,256]{2,1,0:T(8,128)}) %all-gather.57.cloned.1.call-update) | async-done | bytes 2129936 | tf_op jit(solution)/shard_map/all_gather | solution.py:16
  619.1 1.8 reduce_sum.117
  623.6 56.1 %all-gather.35.cloned.1.call-done = f32[32,256,256]{2,1,0:T(8,128)} async-done(((f32[1,256,256]{2,1,0:T(8,128)}), f32[32,256,256]{2,1,0:T(8,128)}) %all-gather.35.cloned.1.call-update) | async-done | bytes 8388624 | tf_op jit(solution)/shard_map/all_gather | solution.py:16
  679.8 3.9 reduce_sum.112
  683.9 11.7 %cholesky.282 = f32[128,128]{1,0:T(8,128)S(1)} custom-call(f32[128,128]{1,0:T(8,128)S(1)} %cholesky.352), custom_call_target="Cholesky" | custom-call | tf_op jit(solution)/shard_map/jit(cholesky)/cholesky | solution.py:63
  695.7 9.8 custom-call.35
  706.0 11.7 %cholesky.299 = f32[128,128]{1,0:T(8,128)S(1)} custom-call(f32[128,128]{1,0:T(8,128)S(1)} %convolution_subtract_fusion.17), custom_call_target="Cholesky" | custom-call | tf_op jit(solution)/shard_map/jit(cholesky)/cholesky | solution.py:63
  720.5 4.3 while.26
  721.3 1.4 bitcast_dynamic-update-slice_fusion.10
  723.3 1.4 bitcast_dynamic-update-slice_fusion.10
  724.8 19.7 %custom-call.36 = f32[2,128,128]{1,2,0:T(8,128)S(1)} custom-call(f32[2,128,128]{2,1,0:T(8,128)S(1)} %get-tuple-element.90), custom_call_target="InvertDiagBlocksLowerTriangular" | custom-call | tf_op jit(solution)/shard_map/triangular_solve/custom-call.0 | solution.py:20
  745.5 56.0 %all-gather.51.cloned.1.call-done = f32[8192,1024]{1,0:T(8,128)} async-done(((f32[256,1024]{1,0:T(8,128)}), f32[8192,1024]{1,0:T(8,128)}) %all-gather.51.cloned.1.call-update) | async-done | bytes 33554448 | tf_op jit(solution)/shard_map/all_gather | solution.py:16
  801.5 11.8 %reduce_sum.113 = f32[256,1024]{1,0:T(8,128)S(1)} reduce(f32[32,256,1024]{2,1,0:T(8,128)} %bitcast.242, f32[]{:T(128)} %constant.178.clone.1), dimensions={0}, to_apply=%region_10.14 | reduce | flops 8126464 | bytes 34603012 | tf_op jit(solution)/shard_map/reduce_sum | solution.py:16
  813.4 1.5 fusion.17
  816.2 2.1 broadcast_select_fusion
  819.7 32.7 %all-gather.59.cloned.1.call-done = f32[32,65,256]{2,1,0:T(8,128)} async-done(((f32[1,65,256]{2,1,0:T(8,128)}), f32[32,65,256]{2,1,0:T(8,128)}) %all-gather.59.cloned.1.call-update) | async-done | bytes 2129936 | tf_op jit(solution)/shard_map/all_gather | solution.py:16
  852.4 1.8 reduce_sum.118
  855.9 39.7 %all-gather.53.cloned.1.call-done = f32[2048,256]{1,0:T(8,128)} async-done(((f32[256,256]{1,0:T(8,128)}), f32[2048,256]{1,0:T(8,128)}) %all-gather.53.cloned.1.call-update) | async-done | bytes 2097168 | tf_op jit(solution)/shard_map/all_gather | solution.py:11
  895.7 1.7 dynamic-slice_select_fusion
  900.1 45.4 %all-gather.61.cloned.1.call-done = f32[32,65,256]{2,1,0:T(8,128)} async-done(((f32[1,65,256]{2,1,0:T(8,128)}), f32[32,65,256]{2,1,0:T(8,128)}) %all-gather.61.cloned.1.call-update) | async-done | bytes 2129936 | tf_op jit(solution)/shard_map/all_gather | solution.py:16
  945.5 1.8 reduce_sum.119
  947.3 58.8 %all-gather.37.cloned.1.call-done = f32[32,256,256]{2,1,0:T(8,128)} async-done(((f32[1,256,256]{2,1,0:T(8,128)}), f32[32,256,256]{2,1,0:T(8,128)}) %all-gather.37.cloned.1.call-update) | async-done | bytes 8388624 | tf_op jit(solution)/shard_map/all_gather | solution.py:16
  1006.2 3.9 reduce_sum.114
  1010.3 11.7 %cholesky.316 = f32[128,128]{1,0:T(8,128)S(1)} custom-call(f32[128,128]{1,0:T(8,128)S(1)} %cholesky.355), custom_call_target="Cholesky" | custom-call | tf_op jit(solution)/shard_map/jit(cholesky)/cholesky | solution.py:63
  1022.1 9.8 custom-call.38
  1032.4 11.7 %cholesky.333 = f32[128,128]{1,0:T(8,128)S(1)} custom-call(f32[128,128]{1,0:T(8,128)S(1)} %convolution_subtract_fusion.16), custom_call_target="Cholesky" | custom-call | tf_op jit(solution)/shard_map/jit(cholesky)/cholesky | solution.py:63
  1046.9 4.2 while.27
  1047.7 1.4 bitcast_dynamic-update-slice_fusion.11
  1051.1 19.7 %custom-call.39 = f32[2,128,128]{1,2,0:T(8,128)S(1)} custom-call(f32[2,128,128]{2,1,0:T(8,128)S(1)} %get-tuple-element.92), custom_call_target="InvertDiagBlocksLowerTriangular" | custom-call | tf_op jit(solution)/shard_map/triangular_solve/custom-call.0 | solution.py:20
  1075.4 52.5 %all-gather.55.cloned.1.call-done = f32[8192,1024]{1,0:T(8,128)} async-done(((f32[256,1024]{1,0:T(8,128)}), f32[8192,1024]{1,0:T(8,128)}) %all-gather.55.cloned.1.call-update) | async-done | bytes 33554448 | tf_op jit(solution)/shard_map/all_gather | solution.py:16
  1127.9 11.8 %reduce_sum.115 = f32[256,1024]{1,0:T(8,128)S(1)} reduce(f32[32,256,1024]{2,1,0:T(8,128)} %bitcast.245, f32[]{:T(128)} %constant.178.clone.1), dimensions={0}, to_apply=%region_14.18 | reduce | flops 8126464 | bytes 34603012 | tf_op jit(solution)/shard_map/reduce_sum | solution.py:16
  1141.6 2.1 fusion.1
  (226 shorter events, 49.4 us)
Async XLA Ops:
  7.2 49.8 %copy-start = (f32[256,1024]{1,0:T(8,128)S(1)}, f32[256,1024]{1,0:T(8,128)}, u32[]{:S(2)}) copy-start(f32[256,1024]{1,0:T(8,128)} %param.11) | copy-start | bytes 3145732
  7.2 48.0 %all-gather.41.cloned.1.call-start = ((), (), s32[]{:S(2)}) async-start(), calls=%async_computation.5 | async-start | bytes 2359296 | tf_op jit(solution)/shard_map/all_gather | solution.py:11
  11.0 103.8 %all-gather.31.cloned.1.call-start = ((), (), s32[]{:S(2)}) async-start(), calls=%async_computation | async-start | bytes 8650752 | tf_op jit(solution)/shard_map/all_gather | solution.py:16
  56.9 179.8 %all-gather.43.cloned.1.call-start = ((), (), s32[]{:S(2)}) async-start(), calls=%async_computation.6 | async-start | bytes 34603008 | tf_op jit(solution)/shard_map/all_gather | solution.py:16
  58.0 235.8 %all-gather.45.cloned.1.call-start = ((), (), s32[]{:S(2)}) async-start(), calls=%async_computation.7 | async-start | bytes 2359296 | tf_op jit(solution)/shard_map/all_gather | solution.py:11
  159.2 90.0 %copy-start.3 = (f32[256,256]{1,0:T(8,128)}, f32[256,256]{1,0:T(8,128)S(1)}, u32[]{:S(2)}) copy-start(f32[256,256]{1,0:T(8,128)S(1)} %get-tuple-element.402) | copy-start | bytes 786436
  178.9 70.9 %copy-start.8 = (f32[2,128,128]{1,2,0:T(8,128)}, f32[2,128,128]{1,2,0:T(8,128)S(1)}, u32[]{:S(2)}) copy-start(f32[2,128,128]{1,2,0:T(8,128)S(1)} %custom-call.30) | copy-start | bytes 393220
  179.9 70.5 %copy-start.5 = (f32[256,128]{0,1:T(8,128)}, f32[256,128]{0,1:T(8,128)S(1)}, u32[]{:S(2)}) copy-start(f32[256,128]{0,1:T(8,128)S(1)} %fusion.65) | copy-start | bytes 393220
  252.4 43.7 %copy-start.17 = (f32[64,256]{1,0:T(8,128)S(1)}, f32[64,256]{1,0:T(8,128)}, u32[]{:S(2)}) copy-start(f32[64,256]{1,0:T(8,128)} %param.14) | copy-start | bytes 196612
  252.5 43.7 %copy-start.20 = (f32[256]{0:T(256)S(1)}, f32[256]{0:T(256)}, u32[]{:S(2)}) copy-start(f32[256]{0:T(256)} %param.13) | copy-start | bytes 3076
  253.2 100.0 %all-gather.33.cloned.1.call-start = ((), (), s32[]{:S(2)}) async-start(), calls=%async_computation.1 | async-start | bytes 8650752 | tf_op jit(solution)/shard_map/all_gather | solution.py:16
  295.5 179.4 %all-gather.47.cloned.1.call-start = ((), (), s32[]{:S(2)}) async-start(), calls=%async_computation.8 | async-start | bytes 34603008 | tf_op jit(solution)/shard_map/all_gather | solution.py:16
  296.1 229.7 %all-gather.39.cloned.1.call-start = ((), (), s32[]{:S(2)}) async-start(), calls=%async_computation.4 | async-start | bytes 2433024 | tf_op jit(solution)/shard_map/all_gather | solution.py:16
  296.8 272.3 %all-gather.49.cloned.1.call-start = ((), (), s32[]{:S(2)}) async-start(), calls=%async_computation.9 | async-start | bytes 2359296 | tf_op jit(solution)/shard_map/all_gather | solution.py:11
  397.9 88.8 %copy-start.23 = (s32[2,2]{1,0:T(2,128)}, s32[2,2]{1,0:T(2,128)S(1)}, u32[]{:S(2)}) copy-start(s32[2,2]{1,0:T(2,128)S(1)} %get-tuple-element.439) | copy-start | bytes 52
  397.9 89.5 %copy-start.4 = (f32[256,256]{1,0:T(8,128)}, f32[256,256]{1,0:T(8,128)S(1)}, u32[]{:S(2)}) copy-start(f32[256,256]{1,0:T(8,128)S(1)} %get-tuple-element.403) | copy-start | bytes 786436
  417.6 70.4 %copy-start.10 = (f32[2,128,128]{1,2,0:T(8,128)}, f32[2,128,128]{1,2,0:T(8,128)S(1)}, u32[]{:S(2)}) copy-start(f32[2,128,128]{1,2,0:T(8,128)S(1)} %custom-call.33) | copy-start | bytes 393220
  490.6 37.0 %copy-start.9 = (f32[2,128,128]{1,2,0:T(8,128)S(1)}, f32[2,128,128]{1,2,0:T(8,128)}, u32[]{:S(2)}) copy-start(f32[2,128,128]{1,2,0:T(8,128)} %copy-done.8) | copy-start | bytes 393220
  490.6 38.5 %copy-start.6 = (f32[256,128]{0,1:T(8,128)S(1)}, f32[256,128]{0,1:T(8,128)}, u32[]{:S(2)}) copy-start(f32[256,128]{0,1:T(8,128)} %copy-done.5) | copy-start | bytes 393220
  490.6 38.6 %copy-start.18 = (f32[64,256]{1,0:T(8,128)S(1)}, f32[64,256]{1,0:T(8,128)}, u32[]{:S(2)}) copy-start(f32[64,256]{1,0:T(8,128)} %param.14) | copy-start | bytes 196612
  491.4 127.7 %all-gather.57.cloned.1.call-start = ((), (), s32[]{:S(2)}) async-start(), calls=%async_computation.13 | async-start | bytes 2433024 | tf_op jit(solution)/shard_map/all_gather | solution.py:16
  492.0 80.3 %copy-start.19 = (s32[4]{0:T(128)S(1)}, s32[4]{0:T(128)}, u32[]{:S(2)}) copy-start(s32[4]{0:T(128)} %param.12) | copy-start | bytes 52
  530.1 90.8 %copy-start.11 = (f32[2,128,128]{1,2,0:T(8,128)S(1)}, f32[2,128,128]{1,2,0:T(8,128)}, u32[]{:S(2)}) copy-start(f32[2,128,128]{1,2,0:T(8,128)} %copy-done.10) | copy-start | bytes 393220
  530.1 149.6 %all-gather.35.cloned.1.call-start = ((), (), s32[]{:S(2)}) async-start(), calls=%async_computation.2 | async-start | bytes 8650752 | tf_op jit(solution)/shard_map/all_gather | solution.py:16
  570.8 230.8 %all-gather.51.cloned.1.call-start = ((), (), s32[]{:S(2)}) async-start(), calls=%async_computation.10 | async-start | bytes 34603008 | tf_op jit(solution)/shard_map/all_gather | solution.py:16
  571.5 280.9 %all-gather.59.cloned.1.call-start = ((), (), s32[]{:S(2)}) async-start(), calls=%async_computation.14 | async-start | bytes 2433024 | tf_op jit(solution)/shard_map/all_gather | solution.py:16
  622.7 61.0 %copy-start.15 = (f32[65,256]{1,0:T(8,128)}, f32[65,256]{1,0:T(8,128)S(1)}, u32[]{:S(2)}) copy-start(f32[65,256]{1,0:T(8,128)S(1)} %fusion.4) | copy-start | bytes 199684
  623.4 272.2 %all-gather.53.cloned.1.call-start = ((), (), s32[]{:S(2)}) async-start(), calls=%async_computation.11 | async-start | bytes 2359296 | tf_op jit(solution)/shard_map/all_gather | solution.py:11
  683.7 36.8 %copy-start.24 = (s32[2,2]{1,0:T(2,128)S(1)}, s32[2,2]{1,0:T(2,128)}, u32[]{:S(2)}) copy-start(s32[2,2]{1,0:T(2,128)} %copy-done.23) | copy-start | bytes 52
  744.4 57.1 %copy-start.12 = (f32[2,128,128]{1,2,0:T(8,128)}, f32[2,128,128]{1,2,0:T(8,128)S(1)}, u32[]{:S(2)}) copy-start(f32[2,128,128]{1,2,0:T(8,128)S(1)} %custom-call.36) | copy-start | bytes 393220
  745.5 109.4 %copy-start.1 = (f32[256,256]{0,1:T(8,128)}, f32[256,256]{0,1:T(8,128)S(1)}, u32[]{:S(2)}) copy-start(f32[256,256]{0,1:T(8,128)S(1)} %maximum_multiply_fusion.7) | copy-start | bytes 786436
  813.4 2.1 copy-start.13
  818.2 36.0 %copy-start.14 = (f32[2,128,128]{1,2,0:T(8,128)S(1)}, f32[2,128,128]{1,2,0:T(8,128)}, u32[]{:S(2)}) copy-start(f32[2,128,128]{1,2,0:T(8,128)} %copy-done.12) | copy-start | bytes 393220
  818.2 36.7 %copy-start.16 = (f32[65,256]{1,0:T(8,128)S(1)}, f32[65,256]{1,0:T(8,128)}, u32[]{:S(2)}) copy-start(f32[65,256]{1,0:T(8,128)} %copy-done.15) | copy-start | bytes 199684
  819.0 126.5 %all-gather.61.cloned.1.call-start = ((), (), s32[]{:S(2)}) async-start(), calls=%async_computation.15 | async-start | bytes 2433024 | tf_op jit(solution)/shard_map/all_gather | solution.py:16
  855.9 150.3 %all-gather.37.cloned.1.call-start = ((), (), s32[]{:S(2)}) async-start(), calls=%async_computation.3 | async-start | bytes 8650752 | tf_op jit(solution)/shard_map/all_gather | solution.py:16
  897.4 230.5 %all-gather.55.cloned.1.call-start = ((), (), s32[]{:S(2)}) async-start(), calls=%async_computation.12 | async-start | bytes 34603008 | tf_op jit(solution)/shard_map/all_gather | solution.py:16
  1010.1 36.8 %copy-start.25 = (s32[2,2]{1,0:T(2,128)S(1)}, s32[2,2]{1,0:T(2,128)}, u32[]{:S(2)}) copy-start(s32[2,2]{1,0:T(2,128)} %copy-done.23) | copy-start | bytes 52
  1010.3 62.2 %copy-start.21 = (f32[256]{0:T(256)S(1)}, f32[256]{0:T(256)}, u32[]{:S(2)}) copy-start(f32[256]{0:T(256)} %convert_element_type.60) | copy-start | bytes 3076
  1022.0 50.5 %copy-start.22 = (pred[256]{0:T(512)(128)(4,1)S(1)}, pred[256]{0:T(512)(128)(4,1)}, u32[]{:S(2)}) copy-start(pred[256]{0:T(512)(128)(4,1)} %broadcast_compare_fusion.2) | copy-start | bytes 772
  1032.1 41.9 %copy-start.2 = (f32[256,256]{0,1:T(8,128)S(1)}, f32[256,256]{0,1:T(8,128)}, u32[]{:S(2)}) copy-start(f32[256,256]{0,1:T(8,128)} %copy-done.1) | copy-start | bytes 786436
  1032.2 41.9 %copy-start.7 = (f32[256,128]{0,1:T(8,128)S(1)}, f32[256,128]{0,1:T(8,128)}, u32[]{:S(2)}) copy-start(f32[256,128]{0,1:T(8,128)} %copy-done.5) | copy-start | bytes 393220
Sparse Core Ops, SparseCore 0:
  11.1 44.0 all-gather.40
  58.3 56.4 all-gather.30
  117.9 118.7 all-gather.42
  253.3 40.3 all-gather.44
  296.7 56.4 all-gather.32
  356.2 118.5 all-gather.46
  477.4 48.3 all-gather.38
  528.2 40.8 all-gather.48
  571.6 47.4 all-gather.56
  622.1 57.6 all-gather.34
  682.9 118.6 all-gather.50
  803.9 48.4 all-gather.58
  854.8 40.8 all-gather.52
  898.0 47.4 all-gather.60
  948.5 57.6 all-gather.36
  1009.2 118.6 all-gather.54
